TPU v7x, 256 devices: a whole 4x4x8 slice. The times are simulated.
256 devices in a mesh: segment: 4 (over y), ctx: 32 (over x_hi, z, core), tp: 2 (over x_lo).
Axes of the slice: x: 4 (x_hi: 2, x_lo: 2; x = x_hi * 2 + x_lo), y: 4, z: 8, core: 2. Of those that a mesh axis runs over, the one named last changes fastest.
Arguments:
- held: bfloat16 [4, 8192, 3584], P('segment', 'ctx'), may hold values from -6 to 6
- text: bfloat16 [8192, 3584], P('ctx'), may hold values from -6 to 6
- frames: bfloat16 [4096, 1024], P('ctx'), may hold values from -6 to 6
- join: int32 [64], P('ctx'), may hold values from 0 to 8128, as said below
- ln_gain: float32 [1024], replicated, may hold values from 0.1 to 1.9
- w_proj: bfloat16 [1024, 3584], P('tp'), may hold values from -0.1875 to 0.1875
- b_proj: float32 [3584], replicated, may hold values from -3 to 3
- norm_gain: float32 [3, 3584], replicated, may hold values from 0.1 to 1.9
- w_qkv: bfloat16 [3, 3584, 2304], P(None, 'ctx', 'tp'), may hold values from -0.09375 to 0.09375
- b_qkv: float32 [3, 2304], P(None, 'tp'), may hold values from -4 to 4
- w_out: bfloat16 [3, 1792, 3584], P(None, 'tp', 'ctx'), may hold values from -1.5 to 1.5
Outputs:
- segment_out: bfloat16 [4, 8192, 3584], P('segment', 'ctx')
Inputs may be any that keep to these rules, and one draw needn't show every extreme that they name: `join`: frames never intersect; the 2 frames f with f // 2 == d lie in order inside positions d * 256 to (d + 1) * 256 - 1.
All inputs are finite; a program needn't handle non-finite values.
Results may differ from a plain program's by a relative error of at most 0.015.
Values may be sent and summed in bfloat16 or wider, within the bound.
No kernel may reach another device: no remote copies, remote signals or barrier semaphores. Data moves between devices by JAX's collectives and lax.ppermute only.
A program may use at most 128 MiB of HBM per device.

v0:
```python
from functools import partial
import jax
import jax.numpy as jnp
from jax import lax
from jax.sharding import PartitionSpec as P

HD = 128
GROUP = 7
FRAME = 64


def shifted(value, axis, by):
    devices = lax.axis_size(axis)
    pairs = [(i, i + by) for i in range(devices) if 0 <= i + by < devices]
    return lax.ppermute(value, axis, pairs)


def update_state(softmax_state, query_flat, query_pos, keys_in, values_in, offset):
    peak_old, total_old, accum_old = softmax_state
    key_pos = jnp.arange(keys_in.shape[0], dtype=jnp.int32)
    scores = jnp.dot(query_flat, keys_in.T, preferred_element_type=jnp.float32) * HD ** (-0.5)
    allowed = key_pos[None, :] <= query_pos[:, None]
    scores = jnp.where(allowed, scores, -1e30)
    peak_new = jnp.maximum(peak_old, jnp.max(scores, axis=1))
    weights = jnp.where(allowed, jnp.exp(scores - peak_new[:, None]), 0.0)
    total_new = jnp.sum(weights, axis=1)
    accum_new = jnp.dot(weights.astype(jnp.bfloat16), values_in, preferred_element_type=jnp.float32)
    return (peak_new, total_new, accum_new)


def keep_state(softmax_state):
    return softmax_state


def on_device(held, text, frames, join, ln_gain, w_proj, b_proj, norm_gain, w_qkv, b_qkv, w_out):
    segment_id = lax.axis_index("segment")
    ctx_id = lax.axis_index("ctx")
    tp_id = lax.axis_index("tp")
    hidden_in = shifted(held[0], "segment", 1)
    tok_rows = hidden_in.shape[0]
    half_rows = tok_rows // 2
    layer_id = jnp.maximum(segment_id - 1, 0)
    weight_qkv = lax.dynamic_index_in_dim(w_qkv, layer_id, 0, keepdims=False)
    bias_qkv = lax.dynamic_index_in_dim(b_qkv, layer_id, 0, keepdims=False)
    layer_gain = lax.dynamic_index_in_dim(norm_gain, layer_id, 0, keepdims=False)
    weight_out = lax.dynamic_index_in_dim(w_out, layer_id, 0, keepdims=False)
    inputs = hidden_in.astype(jnp.float32)
    normed = (
        inputs * lax.rsqrt(jnp.mean(inputs * inputs, axis=1, keepdims=True) + 1e-06) * layer_gain
    ).astype(jnp.bfloat16)
    merged = jnp.dot(
        normed,
        lax.all_gather(weight_qkv, "ctx", axis=0, tiled=True),
        preferred_element_type=jnp.float32,
    )
    merged = (merged + bias_qkv).astype(jnp.bfloat16)
    query_cols = GROUP * HD
    queries = merged[:, :query_cols]
    local_steps = jnp.arange(half_rows, dtype=jnp.int32)
    first_pos = ctx_id * tok_rows + local_steps
    second_q = queries[half_rows:]
    second_pos = ctx_id * tok_rows + half_rows + local_steps
    first_flat = queries[:half_rows].reshape(half_rows * GROUP, HD)
    second_flat = second_q.reshape(half_rows * GROUP, HD)
    first_qpos = jnp.repeat(first_pos, GROUP)
    second_qpos = jnp.repeat(second_pos, GROUP)
    flat_rows = half_rows * GROUP
    empty = (
        jnp.full((flat_rows,), -1e30, jnp.float32),
        jnp.zeros((flat_rows,), jnp.float32),
        jnp.zeros((flat_rows, HD), jnp.float32),
    )
    carried = (empty, empty)
    offset = jnp.int32(0)
    kv_in = lax.all_gather(merged[:, query_cols : query_cols + 2 * HD], "ctx", axis=0, tiled=True)
    keys_in = kv_in[:, :HD]
    values_in = kv_in[:, HD:]
    updated = []
    for softmax_state, query_flat, query_pos in (
        (carried[0], first_flat, first_qpos),
        (carried[1], second_flat, second_qpos),
    ):
        step_fn = partial(
            update_state,
            query_flat=query_flat,
            query_pos=query_pos,
            keys_in=keys_in,
            values_in=values_in,
            offset=offset,
        )
        updated.append(lax.cond(offset <= jnp.max(query_pos), step_fn, keep_state, softmax_state))

    def finish(softmax_state):
        return (
            (softmax_state[2] / softmax_state[1][:, None])
            .astype(jnp.bfloat16)
            .reshape(half_rows, GROUP * HD)
        )

    first_out = finish(updated[0])
    second_out = finish(updated[1])
    attended = jnp.concatenate([first_out, second_out], axis=0)
    partial_model = jnp.dot(
        attended,
        lax.all_gather(weight_out, "ctx", axis=1, tiled=True),
        preferred_element_type=jnp.float32,
    )
    positions = ctx_id * tok_rows + jnp.arange(tok_rows, dtype=jnp.int32)[:, None]
    starts = join[None, :]
    inside = (positions >= starts) & (positions < starts + FRAME)
    frame_base = (jnp.arange(join.shape[0], dtype=jnp.int32) * FRAME)[None, :]
    source = jnp.sum(jnp.where(inside, frame_base + positions - starts, 0), axis=1)
    is_vision = jnp.any(inside, axis=1)

    def vision_term():
        frame_in = frames.astype(jnp.float32)
        center = jnp.mean(frame_in, axis=1, keepdims=True)
        spread = jnp.mean((frame_in - center) * (frame_in - center), axis=1, keepdims=True)
        normed_frames = ((frame_in - center) * lax.rsqrt(spread + 1e-06) * ln_gain).astype(
            jnp.bfloat16
        )
        vis_width = w_proj.shape[0]
        normed_half = lax.dynamic_slice_in_dim(normed_frames, tp_id * vis_width, vis_width, 1)
        projected = jnp.dot(normed_half, w_proj, preferred_element_type=jnp.float32)
        return jnp.where(is_vision[:, None], jnp.take(projected, source, axis=0), 0.0)

    def model_term():
        return partial_model

    is_first = segment_id == 0
    section_term = lax.cond(is_first, vision_term, model_term)
    baseline = jnp.where(
        is_first, jnp.where(is_vision[:, None], b_proj[None, :], text.astype(jnp.float32)), inputs
    )
    own_term = section_term.astype(jnp.bfloat16)
    other_term = lax.ppermute(own_term, "tp", [(0, 1), (1, 0)])
    summed = own_term.astype(jnp.float32) + other_term.astype(jnp.float32)
    result = (baseline + summed).astype(jnp.bfloat16)
    return result[None]


def solution(mesh):
    return jax.shard_map(
        on_device,
        mesh=mesh,
        in_specs=(
            P("segment", "ctx", None),
            P("ctx", None),
            P("ctx", None),
            P("ctx"),
            P(),
            P("tp", None),
            P(),
            P(),
            P(None, "ctx", "tp"),
            P(None, "tp"),
            P(None, "tp", "ctx"),
        ),
        out_specs=P("segment", "ctx", None),
        check_vma=False,
    )
```

profile of v0, /device:TPU:1, one launch (start us, length us, event | category | flops | bytes accessed | tf_op | source)
XLA Modules:
  0.0 367.7 jit_solution(14345656262956970861)
XLA Ops:
  8.5 4.1 %collective-permute-start = (bf16[256,3584]{1,0:T(8,128)(2,1)}, bf16[256,3584]{1,0:T(8,128)(2,1)S(1)}, u32[]{:S(2)}, u32[]{:S(2)}) collective-permute-start(bf16[256,3584]{1,0:T(8,128)(2,1)} %bitcast.20), channel_id=1, source_target_pairs={{0,64},{64,128},{128,192},{1,65},{65,129},{129,193},{2,66},{66,130... | collective-permute-start | bytes 5505032 | tf_op jit(solution)/shard_map/ppermute | solution.py:15
  14.2 37.2 %collective-permute-done = bf16[256,3584]{1,0:T(8,128)(2,1)S(1)} collective-permute-done((bf16[256,3584]{1,0:T(8,128)(2,1)}, bf16[256,3584]{1,0:T(8,128)(2,1)S(1)}, u32[]{:S(2)}, u32[]{:S(2)}) %collective-permute-start) | collective-permute-done | bytes 1835040 | tf_op jit(solution)/shard_map/ppermute | solution.py:15
  51.9 63.3 %all-gather.8.cloned.1.call-done = bf16[1,3584,1152]{2,1,0:T(8,128)(2,1)} async-done(((bf16[1,112,1152]{2,1,0:T(8,128)(2,1)}), bf16[1,3584,1152]{2,1,0:T(8,128)(2,1)}) %all-gather.8.cloned.1.call-update) | async-done | bytes 8257552 | tf_op jit(solution)/shard_map/all_gather | solution.py:53
  115.3 6.8 %fusion.37 = bf16[256,1152]{1,0:T(8,128)(2,1)} fusion(bf16[1,3584,1152]{2,1,0:T(8,128)(2,1)} %all-gather.8.cloned.1.call-done, bf16[256,3584]{1,0:T(8,128)(2,1)S(1)} %collective-permute-done, f32[3584]{0:T(1024)S(1)} %dynamic-slice_reduce_fusion, f32[256]{0:T(256)S(1)} %add_rsqrt_fusion.1, f32[1152]{0:T(1024)S(1)} %dynamic-slice_reduce_fusion.1), kind=kOutput, calls=%fused_computation.56 | convolution fusion | flops 2118189056 | bytes 10702336 | tf_op jit(solution)/shard_map/dot_general | solution.py:51
  122.0 1.6 slice.25
  123.7 1.6 constant_dynamic-slice_fusion
  128.3 78.7 %all-gather.6.cloned.1.call-done = bf16[8192,256]{1,0:T(8,128)(2,1)} async-done(((bf16[256,256]{1,0:T(8,128)(2,1)}), bf16[8192,256]{1,0:T(8,128)(2,1)}) %all-gather.6.cloned.1.call-update) | async-done | bytes 4194320 | tf_op jit(solution)/shard_map/all_gather | solution.py:75
  207.0 3.9 %fusion.49 = (bf16[8192,128]{1,0:T(8,128)(2,1)S(1)}, bf16[8192,128]{1,0:T(8,128)(2,1)}) fusion(bf16[8192,256]{1,0:T(8,128)(2,1)} %all-gather.6.cloned.1.call-done), kind=kLoop, calls=%fused_computation.79 | loop fusion | bytes 8388608 | tf_op jit(solution)/shard_map/slice | solution.py:77
  211.0 42.8 %conditional.3 = (f32[896]{0:T(1024)S(1)}, f32[896,128]{1,0:T(8,128)S(1)}) conditional(s32[]{:T(128)} %convert_element_type.60, () %tuple.37, (s32[128,7]{1,0:T(8,128)S(1)}, bf16[256,1152]{1,0:T(8,128)(2,1)}, bf16[8192,128]{1,0:T(8,128)(2,1)}, bf16[8192,128]{1,0:T(8,128)(2,1)S(1)}) %tuple.38), branch_computations={%region_3.4_spmd, %region_4.7_spmd} | conditional | flops 3875535872 | bytes 93919760 | solution.py:91
  212.4 13.8 %fusion = (f32[896]{0:T(1024)S(1)}, f32[896,8192]{1,0:T(8,128)}) fusion(s32[896]{0:T(1024)S(1)} %le.30, bf16[896,128]{1,0:T(8,128)(2,1)S(1)} %reshape.63, bf16[8192,128]{1,0:T(8,128)(2,1)} %get-tuple-element.49), kind=kOutput, calls=%fused_computation.4 | convolution fusion | flops 1908407424 | bytes 31693824 | tf_op jit(solution)/shard_map/cond/branch_1_fun/dot_general | solution.py:21
  226.2 13.1 %fusion.3 = f32[896,128]{1,0:T(8,128)S(1)} fusion(bf16[8192,128]{1,0:T(8,128)(2,1)S(1)} %get-tuple-element.50, f32[896,8192]{1,0:T(8,128)} %get-tuple-element.92, f32[896]{0:T(1024)S(1)} %broadcast_maximum_fusion, s32[896]{0:T(1024)S(1)} %le.30), kind=kOutput, calls=%fused_computation.7 | convolution fusion | flops 1923088384 | bytes 31923200 | tf_op jit(solution)/shard_map/cond/branch_1_fun/dot_general | solution.py:27
  239.3 14.4 %fusion.2 = f32[896]{0:T(1024)S(1)} fusion(f32[896,8192]{1,0:T(8,128)} %get-tuple-element.92, f32[896]{0:T(1024)S(1)} %broadcast_maximum_fusion, s32[896]{0:T(1024)S(1)} %le.30), kind=kLoop, calls=%fused_computation.6 | loop fusion | flops 44039296 | bytes 29370880 | tf_op jit(solution)/shard_map/cond/branch_1_fun/reduce_sum | solution.py:26
  254.3 43.7 %conditional.4 = (f32[896]{0:T(1024)S(1)}, f32[896,128]{1,0:T(8,128)S(1)}) conditional(s32[]{:T(128)} %convert_element_type.64, () %tuple.39, (s32[128,7]{1,0:T(8,128)S(1)}, bf16[256,1152]{1,0:T(8,128)(2,1)}, bf16[8192,128]{1,0:T(8,128)(2,1)}, bf16[8192,128]{1,0:T(8,128)(2,1)S(1)}) %tuple.40), branch_computations={%region_8.9_spmd, %region_9.12_spmd} | conditional | flops 3875535872 | bytes 93919760 | solution.py:91
  255.9 14.2 %fusion.8 = (f32[896]{0:T(1024)S(1)}, f32[896,8192]{1,0:T(8,128)}) fusion(s32[896]{0:T(1024)S(1)} %le.38, bf16[896,128]{1,0:T(8,128)(2,1)S(1)} %reshape.64, bf16[8192,128]{1,0:T(8,128)(2,1)} %get-tuple-element.53), kind=kOutput, calls=%fused_computation.15 | convolution fusion | flops 1908407424 | bytes 31693824 | tf_op jit(solution)/shard_map/cond/branch_1_fun/dot_general | solution.py:21
  270.1 13.1 %fusion.11 = f32[896,128]{1,0:T(8,128)S(1)} fusion(bf16[8192,128]{1,0:T(8,128)(2,1)S(1)} %get-tuple-element.54, f32[896,8192]{1,0:T(8,128)} %get-tuple-element.94, f32[896]{0:T(1024)S(1)} %broadcast_maximum_fusion.1, s32[896]{0:T(1024)S(1)} %le.38), kind=kOutput, calls=%fused_computation.18 | convolution fusion | flops 1923088384 | bytes 31923200 | tf_op jit(solution)/shard_map/cond/branch_1_fun/dot_general | solution.py:27
  283.2 14.8 %fusion.10 = f32[896]{0:T(1024)S(1)} fusion(f32[896,8192]{1,0:T(8,128)} %get-tuple-element.94, f32[896]{0:T(1024)S(1)} %broadcast_maximum_fusion.1, s32[896]{0:T(1024)S(1)} %le.38), kind=kLoop, calls=%fused_computation.17 | loop fusion | flops 44039296 | bytes 29370880 | tf_op jit(solution)/shard_map/cond/branch_1_fun/reduce_sum | solution.py:26
  298.4 2.6 all-gather.10.cloned.1.call-done
  301.0 6.2 %fusion.27 = bf16[256,3584]{1,0:T(8,128)(2,1)} fusion(bf16[1,896,3584]{1,2,0:T(8,128)(2,1)} %all-gather.10.cloned.1.call-done, bf16[128,896]{1,0:T(8,128)(2,1)S(1)} %reshape.68, bf16[128,896]{1,0:T(8,128)(2,1)S(1)} %reshape.67), kind=kOutput, calls=%fused_computation.45 | convolution fusion | flops 1645084672 | bytes 8716288 | tf_op jit(solution)/shard_map/dot_general | solution.py:103
  307.2 7.3 %conditional.5 = (bf16[256,3584]{1,0:T(8,128)(2,1)}) conditional(s32[]{:T(128)} %convert_element_type.59, bf16[256,3584]{1,0:T(8,128)(2,1)} %fusion.27, (pred[256]{0:T(512)(128)(4,1)S(1)}, pred[256,2]{0,1:T(4,128)(4,1)S(1)}, bf16[128,1024]{1,0:T(8,128)(2,1)S(1)}, f32[1024]{0:T(1024)S(1)}, s32[]{:T(128)}, /*index=5*/bf16[512,3584]{1,0:T(8,128)(2,1)}, ...), branch_computations={%region_13.14_spmd, %region_14.17_spmd} | conditional | flops 472585344 | bytes 13264226 | solution.py:131
  307.6 2.7 fusion.18
  310.5 1.7 gather_fusion
  312.2 2.2 select_select_fusion
  314.8 41.2 %collective-permute-done.1 = bf16[256,3584]{1,0:T(8,128)(2,1)S(1)} collective-permute-done((bf16[256,3584]{1,0:T(8,128)(2,1)}, bf16[256,3584]{1,0:T(8,128)(2,1)S(1)}, u32[]{:S(2)}, u32[]{:S(2)}) %collective-permute-start.1) | collective-permute-done | bytes 1835040 | tf_op jit(solution)/shard_map/ppermute | solution.py:136
  356.0 5.1 %fusion.41 = bf16[1,256,3584]{2,1,0:T(8,128)(2,1)} fusion(bf16[256,3584]{1,0:T(8,128)(2,1)S(1)} %collective-permute-done.1, bf16[256,3584]{1,0:T(8,128)(2,1)} %get-tuple-element.107, bf16[256,3584]{1,0:T(8,128)(2,1)} %copy-done.2, bf16[256,3584]{1,0:T(8,128)(2,1)} %param.18, f32[3584]{0:T(1024)S(1)} %copy-done.4, pred[256]{0:T(512)(128)(4,1)S(1)} %get-tuple-element.89, ...), kind=kLoop, calls=%fused_computation.57 | loop fusion | flops 8257536 | bytes 9189633 | tf_op jit(solution)/shard_map/broadcast_in_dim | solution.py:139
  (60 shorter events, 10.4 us)
Async XLA Ops:
  6.5 1.1 copy-start
  6.5 108.7 %all-gather.8.cloned.1.call-start = ((), (), s32[]{:S(2)}) async-start(), calls=%async_computation.1 | async-start | bytes 8515584 | tf_op jit(solution)/shard_map/all_gather | solution.py:53
  8.4 198.6 %all-gather.6.cloned.1.call-start = ((), (), s32[]{:S(2)}) async-start(), calls=%async_computation | async-start | bytes 4325376 | tf_op jit(solution)/shard_map/all_gather | solution.py:75
  8.5 43.0 %collective-permute-start = (bf16[256,3584]{1,0:T(8,128)(2,1)}, bf16[256,3584]{1,0:T(8,128)(2,1)S(1)}, u32[]{:S(2)}, u32[]{:S(2)}) collective-permute-start(bf16[256,3584]{1,0:T(8,128)(2,1)} %bitcast.20), channel_id=1, source_target_pairs={{0,64},{64,128},{128,192},{1,65},{65,129},{129,193},{2,66},{66,130... | collective-permute-start | bytes 5505032 | tf_op jit(solution)/shard_map/ppermute | solution.py:15
  51.5 70.6 %copy-start.2 = (bf16[256,3584]{1,0:T(8,128)(2,1)}, bf16[256,3584]{1,0:T(8,128)(2,1)S(1)}, u32[]{:S(2)}) copy-start(bf16[256,3584]{1,0:T(8,128)(2,1)S(1)} %collective-permute-done) | copy-start | bytes 5505028
  51.9 76.2 %copy-start.5 = (s32[2]{0:T(128)S(1)}, s32[2]{0:T(128)}, u32[]{:S(2)}) copy-start(s32[2]{0:T(128)} %param.20) | copy-start | bytes 28
  123.6 177.4 %all-gather.10.cloned.1.call-start = ((), (), s32[]{:S(2)}) async-start(), calls=%async_computation.2 | async-start | bytes 6623232 | tf_op jit(solution)/shard_map/all_gather | solution.py:105
  254.3 46.8 %copy-start.3 = (bf16[128,1024]{1,0:T(8,128)(2,1)S(1)}, bf16[128,1024]{1,0:T(8,128)(2,1)}, u32[]{:S(2)}) copy-start(bf16[128,1024]{1,0:T(8,128)(2,1)} %param.19) | copy-start | bytes 786436
  254.3 46.7 %copy-start.6 = (f32[1024]{0:T(1024)S(1)}, f32[1024]{0:T(1024)}, u32[]{:S(2)}) copy-start(f32[1024]{0:T(1024)} %param.21) | copy-start | bytes 12292
  307.2 48.8 %copy-start.4 = (f32[3584]{0:T(1024)S(1)}, f32[3584]{0:T(1024)}, u32[]{:S(2)}) copy-start(f32[3584]{0:T(1024)} %param.23) | copy-start | bytes 43012
  314.5 46.7 %copy-start.1 = (bf16[3,112,1152]{2,1,0:T(8,128)(2,1)S(1)}, bf16[3,112,1152]{2,1,0:T(8,128)(2,1)}, u32[]{:S(2)}) copy-start(bf16[3,112,1152]{2,1,0:T(8,128)(2,1)} %param.25) | copy-start | bytes 2322436
  314.5 41.6 %collective-permute-start.1 = (bf16[256,3584]{1,0:T(8,128)(2,1)}, bf16[256,3584]{1,0:T(8,128)(2,1)S(1)}, u32[]{:S(2)}, u32[]{:S(2)}) collective-permute-start(bf16[256,3584]{1,0:T(8,128)(2,1)} %get-tuple-element.107), channel_id=1, source_target_pairs={{0,1},{1,0},{2,3},{3,2},{4,5},{5,4},{6,7},{7,6},{8,9},{9,8},{10,11... | collective-permute-start | bytes 5505032 | tf_op jit(solution)/shard_map/ppermute | solution.py:136
Sparse Core Ops, SparseCore 0:
  10.0 105.1 all-gather.7
  123.7 83.2 all-gather.5
  209.7 91.2 all-gather.9
where the time goes:
time: 369 us; the launch traced here: 368 us
  waiting for transfers between devices  223 us (60%)
  matrix products  69.9 us (19%)
  other arithmetic  39.4 us (11%)
  local copies, waits for them, and re-layouts  15.9 us (4%)
  between operations  14.5 us (4%)
  starting transfers between devices  4.56 us (1%)
    all_gather x1, waiting for transfers between devices, on_device(): lax.all_gather(merged[:, query_cols:query_cols + 2 * HD], 'ctx', axis=0,...  78.7 us
    all_gather x1, waiting for transfers between devices, on_device(): lax.all_gather(weight_qkv, 'ctx', axis=0, tiled=True)  63.3 us
    ppermute x1, waiting for transfers between devices, on_device(): other_term = lax.ppermute(own_term, 'tp', [(0, 1), (1, 0)])  41.2 us
    ppermute x1, waiting for transfers between devices, shifted(): return lax.ppermute(value, axis, pairs)  37.2 us
    reduce_sum x2, other arithmetic, update_state(): total_new = jnp.sum(weights, axis=1)  29.2 us
    dot_general x2, matrix products, update_state(): jnp.dot(query_flat, keys_in.T, preferred_element_type=jnp.float32)  28 us
    dot_general x2, matrix products, update_state(): jnp.dot(weights.astype(jnp.bfloat16), values_in, preferred_element_type=j...  26.2 us
  transfers between devices with their start and end apart: 5, of which 5 were waited for; matrix products, arithmetic and copies ran while one was open for 26% of the time, Pallas kernels for 0%

commit v1 on v0

--- a/solution.py
+++ b/solution.py
@@ -50,7 +50,9 @@
     ).astype(jnp.bfloat16)
     merged = jnp.dot(
         normed,
-        lax.all_gather(weight_qkv, "ctx", axis=0, tiled=True),
+        jnp.concatenate(
+            lax.all_to_all(jnp.stack([weight_qkv] * lax.axis_size("ctx")), "ctx", 0, 0), axis=0
+        ),
         preferred_element_type=jnp.float32,
     )
     merged = (merged + bias_qkv).astype(jnp.bfloat16)

time: 369 us -> 466 us (1.26)
  waiting for transfers between devices: 223 us -> 305 us
  starting transfers between devices: 4.56 us -> 16.3 us
    all_to_all x0 -> x1, waiting for transfers between devices: none -> 140 us  [on_device(): lax.all_to_all(jnp.stack([weight_qkv] * lax.axis_size('ctx')), 'ctx', 0, 0)]
    all_gather x1 -> x0, waiting for transfers between devices: 63.3 us -> none  [on_device(): lax.all_gather(weight_qkv, 'ctx', axis=0, tiled=True)]
    all_to_all x0 -> x1, starting transfers between devices: none -> 12.6 us  [on_device(): lax.all_to_all(jnp.stack([weight_qkv] * lax.axis_size('ctx')), 'ctx', 0, 0)]
    all_gather x1, waiting for transfers between devices: 78.7 us -> 84.1 us  [on_device(): lax.all_gather(merged[:, query_cols:query_cols + 2 * HD], 'ctx', axis=0,...]
  transfers between devices with their start and end apart: 5 -> 5, of which waited for: 5 -> 5; matrix products, arithmetic and copies ran while one was open for 26% -> 21% of each run, Pallas kernels for 0% -> 0%
where the time goes in v1:
time: 466 us; the launch traced here: 465 us
  waiting for transfers between devices  305 us (65%)
  matrix products  69.7 us (15%)
  other arithmetic  39.4 us (8%)
  local copies, waits for them, and re-layouts  18.9 us (4%)
  starting transfers between devices  16.3 us (3%)
  between operations  14.8 us (3%)
    all_to_all x1, waiting for transfers between devices, on_device(): lax.all_to_all(jnp.stack([weight_qkv] * lax.axis_size('ctx')), 'ctx', 0, 0)  140 us
    all_gather x1, waiting for transfers between devices, on_device(): lax.all_gather(merged[:, query_cols:query_cols + 2 * HD], 'ctx', axis=0,...  84.1 us
    ppermute x1, waiting for transfers between devices, on_device(): other_term = lax.ppermute(own_term, 'tp', [(0, 1), (1, 0)])  41.3 us
    ppermute x1, waiting for transfers between devices, shifted(): return lax.ppermute(value, axis, pairs)  37.7 us
    reduce_sum x2, other arithmetic, update_state(): total_new = jnp.sum(weights, axis=1)  29.2 us
    dot_general x2, matrix products, update_state(): jnp.dot(query_flat, keys_in.T, preferred_element_type=jnp.float32)  27.8 us
    dot_general x2, matrix products, update_state(): jnp.dot(weights.astype(jnp.bfloat16), values_in, preferred_element_type=j...  26.2 us
    all_to_all x1, starting transfers between devices, on_device(): lax.all_to_all(jnp.stack([weight_qkv] * lax.axis_size('ctx')), 'ctx', 0, 0)  12.6 us
  transfers between devices with their start and end apart: 5, of which 5 were waited for; matrix products, arithmetic and copies ran while one was open for 21% of the time, Pallas kernels for 0%

profile of v1, /device:TPU:1, one launch (start us, length us, event | category | flops | bytes accessed | tf_op | source)
XLA Modules:
  0.0 465.0 jit_solution(17341451175194634249)
XLA Ops:
  7.7 3.8 stack.2
  11.5 12.6 %all-to-all-start = ((bf16[32,112,1152]{2,1,0:T(8,128)(2,1)}), bf16[32,112,1152]{2,1,0:T(8,128)(2,1)}, u32[]{:S(2)}, u32[]{:S(2)}) async-start(bf16[32,112,1152]{2,1,0:T(8,128)(2,1)} %stack.2), calls=%async_computation | async-start | bytes 16515072 | tf_op jit(solution)/shard_map/all_to_all | solution.py:54
  24.2 3.3 collective-permute-start
  29.1 37.7 %collective-permute-done = bf16[256,3584]{1,0:T(8,128)(2,1)S(1)} collective-permute-done((bf16[256,3584]{1,0:T(8,128)(2,1)}, bf16[256,3584]{1,0:T(8,128)(2,1)S(1)}, u32[]{:S(2)}, u32[]{:S(2)}) %collective-permute-start) | collective-permute-done | bytes 1835040 | tf_op jit(solution)/shard_map/ppermute | solution.py:15
  67.2 139.7 %all-to-all-done = bf16[32,112,1152]{2,1,0:T(8,128)(2,1)} async-done(((bf16[32,112,1152]{2,1,0:T(8,128)(2,1)}), bf16[32,112,1152]{2,1,0:T(8,128)(2,1)}, u32[]{:S(2)}, u32[]{:S(2)}) %all-to-all-start) | async-done | bytes 8257568 | tf_op jit(solution)/shard_map/all_to_all | solution.py:54
  206.9 6.8 %fusion.32 = bf16[256,1152]{1,0:T(8,128)(2,1)} fusion(bf16[3584,1152]{1,0:T(8,128)(2,1)} %bitcast.2, bf16[256,3584]{1,0:T(8,128)(2,1)S(1)} %collective-permute-done, f32[3584]{0:T(1024)S(1)} %dynamic-slice_reduce_fusion, f32[256]{0:T(256)S(1)} %add_rsqrt_fusion.1, f32[1152]{0:T(1024)S(1)} %dynamic-slice_reduce_fusion.1), kind=kOutput, calls=%fused_computation.54 | convolution fusion | flops 2118189056 | bytes 10702336 | tf_op jit(solution)/shard_map/dot_general | solution.py:51
  220.0 84.1 %all-gather.4.cloned.1.call-done = bf16[8192,256]{1,0:T(8,128)(2,1)} async-done(((bf16[256,256]{1,0:T(8,128)(2,1)}), bf16[8192,256]{1,0:T(8,128)(2,1)}) %all-gather.4.cloned.1.call-update) | async-done | bytes 4194320 | tf_op jit(solution)/shard_map/all_gather | solution.py:77
  304.1 3.9 fusion.42
  308.0 42.9 %conditional.3 = (f32[896]{0:T(1024)S(1)}, f32[896,128]{1,0:T(8,128)S(1)}) conditional(s32[]{:T(128)} %convert_element_type.60, () %tuple.37, (s32[128,7]{1,0:T(8,128)S(1)}, bf16[256,1152]{1,0:T(8,128)(2,1)}, bf16[8192,128]{1,0:T(8,128)(2,1)}, bf16[8192,128]{1,0:T(8,128)(2,1)S(1)}) %tuple.38), branch_computations={%region_3.4_spmd, %region_4.7_spmd} | conditional | flops 3875535872 | bytes 93919760 | solution.py:93
  309.6 13.8 %fusion = (f32[896]{0:T(1024)S(1)}, f32[896,8192]{1,0:T(8,128)}) fusion(s32[896]{0:T(1024)S(1)} %le.30, bf16[896,128]{1,0:T(8,128)(2,1)S(1)} %reshape.66, bf16[8192,128]{1,0:T(8,128)(2,1)} %get-tuple-element.49), kind=kOutput, calls=%fused_computation.4 | convolution fusion | flops 1908407424 | bytes 31693824 | tf_op jit(solution)/shard_map/cond/branch_1_fun/dot_general | solution.py:21
  323.5 13.1 %fusion.3 = f32[896,128]{1,0:T(8,128)S(1)} fusion(bf16[8192,128]{1,0:T(8,128)(2,1)S(1)} %get-tuple-element.50, f32[896,8192]{1,0:T(8,128)} %get-tuple-element.92, f32[896]{0:T(1024)S(1)} %broadcast_maximum_fusion, s32[896]{0:T(1024)S(1)} %le.30), kind=kOutput, calls=%fused_computation.7 | convolution fusion | flops 1923088384 | bytes 31923200 | tf_op jit(solution)/shard_map/cond/branch_1_fun/dot_general | solution.py:27
  336.5 14.4 %fusion.2 = f32[896]{0:T(1024)S(1)} fusion(f32[896,8192]{1,0:T(8,128)} %get-tuple-element.92, f32[896]{0:T(1024)S(1)} %broadcast_maximum_fusion, s32[896]{0:T(1024)S(1)} %le.30), kind=kLoop, calls=%fused_computation.6 | loop fusion | flops 44039296 | bytes 29370880 | tf_op jit(solution)/shard_map/cond/branch_1_fun/reduce_sum | solution.py:26
  351.5 43.5 %conditional.4 = (f32[896]{0:T(1024)S(1)}, f32[896,128]{1,0:T(8,128)S(1)}) conditional(s32[]{:T(128)} %convert_element_type.64, () %tuple.39, (s32[128,7]{1,0:T(8,128)S(1)}, bf16[256,1152]{1,0:T(8,128)(2,1)}, bf16[8192,128]{1,0:T(8,128)(2,1)}, bf16[8192,128]{1,0:T(8,128)(2,1)S(1)}) %tuple.40), branch_computations={%region_8.9_spmd, %region_9.12_spmd} | conditional | flops 3875535872 | bytes 93919760 | solution.py:93
  353.2 14.0 %fusion.8 = (f32[896]{0:T(1024)S(1)}, f32[896,8192]{1,0:T(8,128)}) fusion(s32[896]{0:T(1024)S(1)} %le.38, bf16[896,128]{1,0:T(8,128)(2,1)S(1)} %reshape.67, bf16[8192,128]{1,0:T(8,128)(2,1)} %get-tuple-element.53), kind=kOutput, calls=%fused_computation.15 | convolution fusion | flops 1908407424 | bytes 31693824 | tf_op jit(solution)/shard_map/cond/branch_1_fun/dot_general | solution.py:21
  367.2 13.1 %fusion.11 = f32[896,128]{1,0:T(8,128)S(1)} fusion(bf16[8192,128]{1,0:T(8,128)(2,1)S(1)} %get-tuple-element.54, f32[896,8192]{1,0:T(8,128)} %get-tuple-element.94, f32[896]{0:T(1024)S(1)} %broadcast_maximum_fusion.1, s32[896]{0:T(1024)S(1)} %le.38), kind=kOutput, calls=%fused_computation.18 | convolution fusion | flops 1923088384 | bytes 31923200 | tf_op jit(solution)/shard_map/cond/branch_1_fun/dot_general | solution.py:27
  380.3 14.8 %fusion.10 = f32[896]{0:T(1024)S(1)} fusion(f32[896,8192]{1,0:T(8,128)} %get-tuple-element.94, f32[896]{0:T(1024)S(1)} %broadcast_maximum_fusion.1, s32[896]{0:T(1024)S(1)} %le.38), kind=kLoop, calls=%fused_computation.17 | loop fusion | flops 44039296 | bytes 29370880 | tf_op jit(solution)/shard_map/cond/branch_1_fun/reduce_sum | solution.py:26
  395.5 2.5 all-gather.6.cloned.1.call-done
  398.1 6.2 %fusion.25 = bf16[256,3584]{1,0:T(8,128)(2,1)} fusion(bf16[1,896,3584]{1,2,0:T(8,128)(2,1)} %all-gather.6.cloned.1.call-done, bf16[128,896]{1,0:T(8,128)(2,1)S(1)} %reshape.73, bf16[128,896]{1,0:T(8,128)(2,1)S(1)} %reshape.72), kind=kOutput, calls=%fused_computation.43 | convolution fusion | flops 1645084672 | bytes 8716288 | tf_op jit(solution)/shard_map/dot_general | solution.py:105
  404.2 7.3 %conditional.5 = (bf16[256,3584]{1,0:T(8,128)(2,1)}) conditional(s32[]{:T(128)} %convert_element_type.59, bf16[256,3584]{1,0:T(8,128)(2,1)} %fusion.25, (pred[256]{0:T(512)(128)(4,1)S(1)}, pred[256,2]{0,1:T(4,128)(4,1)S(1)}, bf16[128,1024]{1,0:T(8,128)(2,1)S(1)}, f32[1024]{0:T(1024)S(1)}, s32[]{:T(128)}, /*index=5*/bf16[512,3584]{1,0:T(8,128)(2,1)}, ...), branch_computations={%region_13.14_spmd, %region_14.17_spmd} | conditional | flops 472585344 | bytes 13264226 | solution.py:133
  404.7 2.7 fusion.18
  407.5 1.7 gather_fusion
  409.3 2.2 select_select_fusion
  411.8 41.3 %collective-permute-done.1 = bf16[256,3584]{1,0:T(8,128)(2,1)S(1)} collective-permute-done((bf16[256,3584]{1,0:T(8,128)(2,1)}, bf16[256,3584]{1,0:T(8,128)(2,1)S(1)}, u32[]{:S(2)}, u32[]{:S(2)}) %collective-permute-start.1) | collective-permute-done | bytes 1835040 | tf_op jit(solution)/shard_map/ppermute | solution.py:138
  453.1 5.1 %fusion.34 = bf16[1,256,3584]{2,1,0:T(8,128)(2,1)} fusion(bf16[256,3584]{1,0:T(8,128)(2,1)S(1)} %collective-permute-done.1, bf16[256,3584]{1,0:T(8,128)(2,1)} %get-tuple-element.107, bf16[256,3584]{1,0:T(8,128)(2,1)} %copy-done.2, bf16[256,3584]{1,0:T(8,128)(2,1)} %param.18, f32[3584]{0:T(1024)S(1)} %copy-done.4, pred[256]{0:T(512)(128)(4,1)S(1)} %get-tuple-element.89, ...), kind=kLoop, calls=%fused_computation.55 | loop fusion | flops 8257536 | bytes 9189633 | tf_op jit(solution)/shard_map/broadcast_in_dim | solution.py:141
  (60 shorter events, 12.9 us)
Async XLA Ops:
  6.5 1.1 copy-start
  11.5 195.4 %all-to-all-start = ((bf16[32,112,1152]{2,1,0:T(8,128)(2,1)}), bf16[32,112,1152]{2,1,0:T(8,128)(2,1)}, u32[]{:S(2)}, u32[]{:S(2)}) async-start(bf16[32,112,1152]{2,1,0:T(8,128)(2,1)} %stack.2), calls=%async_computation | async-start | bytes 16515072 | tf_op jit(solution)/shard_map/all_to_all | solution.py:54
  24.1 280.0 %all-gather.4.cloned.1.call-start = ((), (), s32[]{:S(2)}) async-start(), calls=%async_computation.1 | async-start | bytes 4325376 | tf_op jit(solution)/shard_map/all_gather | solution.py:77
  24.2 42.6 %collective-permute-start = (bf16[256,3584]{1,0:T(8,128)(2,1)}, bf16[256,3584]{1,0:T(8,128)(2,1)S(1)}, u32[]{:S(2)}, u32[]{:S(2)}) collective-permute-start(bf16[256,3584]{1,0:T(8,128)(2,1)} %bitcast.17), channel_id=1, source_target_pairs={{0,64},{64,128},{128,192},{1,65},{65,129},{129,193},{2,66},{66,130... | collective-permute-start | bytes 5505032 | tf_op jit(solution)/shard_map/ppermute | solution.py:15
  66.8 146.9 %copy-start.2 = (bf16[256,3584]{1,0:T(8,128)(2,1)}, bf16[256,3584]{1,0:T(8,128)(2,1)S(1)}, u32[]{:S(2)}) copy-start(bf16[256,3584]{1,0:T(8,128)(2,1)S(1)} %collective-permute-done) | copy-start | bytes 5505028
  206.9 12.9 %copy-start.5 = (s32[2]{0:T(128)S(1)}, s32[2]{0:T(128)}, u32[]{:S(2)}) copy-start(s32[2]{0:T(128)} %param.20) | copy-start | bytes 28
  215.3 182.8 %all-gather.6.cloned.1.call-start = ((), (), s32[]{:S(2)}) async-start(), calls=%async_computation.2 | async-start | bytes 6623232 | tf_op jit(solution)/shard_map/all_gather | solution.py:107
  351.5 46.5 %copy-start.3 = (bf16[128,1024]{1,0:T(8,128)(2,1)S(1)}, bf16[128,1024]{1,0:T(8,128)(2,1)}, u32[]{:S(2)}) copy-start(bf16[128,1024]{1,0:T(8,128)(2,1)} %param.19) | copy-start | bytes 786436
  351.5 46.5 %copy-start.6 = (f32[1024]{0:T(1024)S(1)}, f32[1024]{0:T(1024)}, u32[]{:S(2)}) copy-start(f32[1024]{0:T(1024)} %param.21) | copy-start | bytes 12292
  404.2 48.8 %copy-start.4 = (f32[3584]{0:T(1024)S(1)}, f32[3584]{0:T(1024)}, u32[]{:S(2)}) copy-start(f32[3584]{0:T(1024)} %param.23) | copy-start | bytes 43012
  411.5 46.7 %copy-start.1 = (bf16[3,112,1152]{2,1,0:T(8,128)(2,1)S(1)}, bf16[3,112,1152]{2,1,0:T(8,128)(2,1)}, u32[]{:S(2)}) copy-start(bf16[3,112,1152]{2,1,0:T(8,128)(2,1)} %param.25) | copy-start | bytes 2322436
  411.5 41.6 %collective-permute-start.1 = (bf16[256,3584]{1,0:T(8,128)(2,1)}, bf16[256,3584]{1,0:T(8,128)(2,1)S(1)}, u32[]{:S(2)}, u32[]{:S(2)}) collective-permute-start(bf16[256,3584]{1,0:T(8,128)(2,1)} %get-tuple-element.107), channel_id=1, source_target_pairs={{0,1},{1,0},{2,3},{3,2},{4,5},{5,4},{6,7},{7,6},{8,9},{9,8},{10,11... | collective-permute-start | bytes 5505032 | tf_op jit(solution)/shard_map/ppermute | solution.py:138
Sparse Core Ops, SparseCore 0:
  215.4 88.6 all-gather.3
  306.8 91.2 all-gather.5
